TPU v7x, 256 devices: a whole 4x4x8 slice. The times are simulated.
256 devices in a mesh: dp: 32 (over y, x, core), tensor: 8 (over z).
Axes of the slice: x: 4, y: 4, z: 8, core: 2. Of those that a mesh axis runs over, the one named last changes fastest.
Arguments:
- tokens: bfloat16 [8192, 8192], P('dp'), may hold values from -6 to 6
- router_weight: bfloat16 [8192, 32], replicated, may hold values from -0.0625 to 0.0625
- gate_weight: bfloat16 [14336, 8192], P(('dp', 'tensor')), may hold values from -0.0625 to 0.0625
- up_weight: bfloat16 [14336, 8192], P(('dp', 'tensor')), may hold values from -0.0625 to 0.0625
- down_weight: bfloat16 [14336, 8192], P(('dp', 'tensor')), may hold values from -0.25 to 0.25
- cluster_of: int32 [14336, 1], P('dp'), may hold values from 0 to 31; in each aligned block of 448 rows (0 to 447, 448 to 895, ...) at most 28 rows name the same one
- expert_ids: int32 [8192, 2], P('dp'), may hold values from 0 to 31, all different within a row; in each aligned block of 256 rows (0 to 255, 256 to 511, ...) at most 32 rows name the same one
Outputs:
- mixed_out: bfloat16 [8192, 8192], P('dp', 'tensor')
Inputs may be any that keep to these rules, and one draw needn't show every extreme that they name: `expert_ids`: in each aligned block of 256 rows (the tokens of one dp index) no expert is named by more than 32 rows, a bound that some block reaches; a row names two different experts; every expert is named somewhere. `cluster_of`: in each aligned block of 448 hidden units no cluster holds more than 28 units, and some cluster holds exactly 28; every cluster holds some unit.
All inputs are finite; a program needn't handle non-finite values.
Results may differ from a plain program's by a relative error of at most 0.023.
Values may be sent and summed in bfloat16 or wider, within the bound.
No kernel may reach another device: no remote copies, remote signals or barrier semaphores. Data moves between devices by JAX's collectives and lax.ppermute only.
A program may use at most 64 MiB of HBM per device.

v0:
```python
import jax
import jax.numpy as jnp
from jax import lax
from jax.sharding import PartitionSpec as P


def place_rows(labels, bin_count, capacity):
    count_rows = labels.shape[0]
    onehot = (labels[:, None] == jnp.arange(bin_count, dtype=jnp.int32)[None, :]).astype(jnp.int32)
    before = jnp.cumsum(onehot, axis=0) - onehot
    rank_in = jnp.sum(before * onehot, axis=1)
    position = labels * capacity + rank_in
    slot_list = jnp.full((bin_count * capacity,), count_rows, jnp.int32)
    slot_list = slot_list.at[position].set(jnp.arange(count_rows, dtype=jnp.int32))
    return (slot_list, position)


def with_zero_row(matrix):
    pad = jnp.zeros((1,) + matrix.shape[1:], matrix.dtype)
    return jnp.concatenate([matrix, pad], axis=0)


def against(left_side, right_side):
    return lax.dot_general(
        left_side, right_side, (((1,), (1,)), ((), ())), preferred_element_type=jnp.float32
    )


def on_device(tokens, router_weight, gate_weight, up_weight, down_weight, cluster_of, expert_ids):
    owners = lax.axis_size("dp")
    tensor_count = lax.axis_size("tensor")
    width_part = tokens.shape[1] // tensor_count
    token_count = tokens.shape[0]
    logits = jnp.dot(tokens, router_weight, preferred_element_type=jnp.float32)
    scores = jax.nn.sigmoid(jnp.take_along_axis(logits, expert_ids, axis=1))
    mixing = scores / jnp.sum(scores, axis=1, keepdims=True)
    stacked = jnp.stack([gate_weight, up_weight, down_weight], axis=1)
    rows = lax.all_to_all(stacked, "tensor", split_axis=2, concat_axis=0, tiled=True)
    unit_cap = 2 * rows.shape[0] // owners
    unit_list, unit_spot = place_rows(cluster_of[:, 0], owners, unit_cap)
    pick = with_zero_row(rows)[unit_list]
    own = lax.all_to_all(pick, "dp", split_axis=0, concat_axis=0, tiled=True)
    capacity = 4 * token_count // owners
    flat_ids = expert_ids.reshape(-1)
    slot_list, slot_spot = place_rows(flat_ids, owners, capacity)
    features = lax.dynamic_slice_in_dim(
        tokens, lax.axis_index("tensor") * width_part, width_part, 1
    )
    outgoing = with_zero_row(features)[slot_list // 2]
    arrived = lax.all_to_all(outgoing, "dp", split_axis=0, concat_axis=0, tiled=True)
    gate_part = against(arrived, own[:, 0, :]).astype(jnp.bfloat16)
    up_part = against(arrived, own[:, 1, :]).astype(jnp.bfloat16)
    both = jnp.stack([gate_part, up_part], axis=1)
    summed = lax.psum_scatter(both, "tensor", scatter_dimension=0, tiled=True).astype(jnp.float32)
    hidden_part = (jax.nn.silu(summed[:, 0, :]) * summed[:, 1, :]).astype(jnp.bfloat16)
    hidden = lax.all_gather(hidden_part, "tensor", axis=0, tiled=True)
    expert_out = jnp.dot(hidden, own[:, 2, :], preferred_element_type=jnp.float32).astype(
        jnp.bfloat16
    )
    returned = lax.all_to_all(expert_out, "dp", split_axis=0, concat_axis=0, tiled=True)
    picked_out = returned[slot_spot].reshape(token_count, 2, width_part)
    mixed_out = jnp.sum(mixing[:, :, None] * picked_out.astype(jnp.float32), axis=1)
    return mixed_out.astype(jnp.bfloat16)


def solution(mesh):
    in_specs = (
        P("dp", None),
        P(),
        P(("dp", "tensor"), None),
        P(("dp", "tensor"), None),
        P(("dp", "tensor"), None),
        P("dp", None),
        P("dp", None),
    )
    out_specs = P("dp", "tensor")
    return jax.shard_map(
        on_device, mesh=mesh, in_specs=in_specs, out_specs=out_specs, check_vma=False
    )
```

profile of v0, /device:TPU:1, one launch (start us, length us, event | category | flops | bytes accessed | tf_op | source)
XLA Modules:
  0.0 451.2 jit_solution(5226104023529939072)
XLA Ops:
  6.5 2.1 pad_maximum_fusion.1
  8.6 8.4 %copy.72 = bf16[56,3,8192]{0,1,2:T(4,128)(2,1)} copy(bf16[56,3,8192]{2,0,1:T(8,128)(2,1)S(1)} %pad_maximum_fusion.1) | data formatting | bytes 5505024 | tf_op jit(solution)/shard_map/stack | solution.py:37
  17.0 12.4 %reshape.154 = bf16[8,2,86016]{2,1,0:T(2,128)(2,1)} reshape(bf16[8192,3,56]{2,1,0:T(4,128)(2,1)} %bitcast.87) | data formatting | bytes 5505024
  29.4 9.1 %all-to-all-start.1 = ((bf16[8,2,86016]{2,1,0:T(2,128)(2,1)}), bf16[8,2,86016]{2,1,0:T(2,128)(2,1)S(1)}, u32[]{:S(2)}, u32[]{:S(2)}) async-start(bf16[8,2,86016]{2,1,0:T(2,128)(2,1)} %reshape.154), calls=%async_computation.1 | async-start | bytes 5505024 | tf_op jit(solution)/shard_map/all_to_all | solution.py:38
  38.6 1.2 reduce-window.16
  39.7 0.2 slice_reduce_fusion
  40.2 2.9 scatter_custom_fusion.1
  43.1 61.2 %all-to-all-done.1 = bf16[8,2,86016]{2,1,0:T(2,128)(2,1)S(1)} async-done(((bf16[8,2,86016]{2,1,0:T(2,128)(2,1)}), bf16[8,2,86016]{2,1,0:T(2,128)(2,1)S(1)}, u32[]{:S(2)}, u32[]{:S(2)}) %all-to-all-start.1) | async-done | bytes 2752544 | tf_op jit(solution)/shard_map/all_to_all | solution.py:38
  104.3 13.2 %reshape.155 = bf16[8192,3,56]{2,1,0:T(4,128)(2,1)} reshape(bf16[8,2,86016]{2,1,0:T(2,128)(2,1)S(1)} %all-to-all-done.1) | data formatting | bytes 5505024
  117.5 10.6 %copy.79 = bf16[56,3,8,1024]{3,0,2,1:T(8,128)(2,1)S(1)} copy(bf16[56,3,8,1024]{0,1,3,2:T(4,128)(2,1)} %bitcast.88) | data formatting | bytes 5505024 | tf_op jit(solution)/shard_map/all_to_all | solution.py:38
  128.1 2.4 copy.75
  130.5 3.2 concatenate.7
  133.7 33.1 %gather_fusion.1 = bf16[896,3,1024]{2,1,0:T(4,128)(2,1)} fusion(bf16[449,3,1024]{2,1,0:T(4,128)(2,1)} %concatenate.7, s32[1024]{0:T(1024)S(1)} %pad_clamp_fusion.1), kind=kCustom, calls=%fused_computation.1 | custom fusion | bytes 11013632 | tf_op jit(solution)/shard_map/gather | solution.py:41
  166.8 7.6 %all-to-all-start.2 = ((bf16[896,3,1024]{2,1,0:T(4,128)(2,1)}), bf16[896,3,1024]{2,1,0:T(4,128)(2,1)}, u32[]{:S(2)}, u32[]{:S(2)}) async-start(bf16[896,3,1024]{2,1,0:T(4,128)(2,1)} %gather_fusion.1), calls=%async_computation.2 | async-start | bytes 14680064 | tf_op jit(solution)/shard_map/all_to_all | solution.py:42
  174.4 0.1 copy.69
  174.6 0.1 eq.51
  174.7 0.1 eq.47
  174.9 1.1 constant_dynamic-slice_fusion
  176.0 1.2 reduce-window.14
  177.2 0.2 slice_reduce_fusion.1
  177.5 0.1 copy.68
  177.6 0.1 mul.48
  177.8 0.1 fusion.16
  177.9 2.4 scatter_custom_fusion
  180.4 5.4 %gather_fusion = bf16[1024,1024]{1,0:T(8,128)(2,1)} fusion(bf16[257,1024]{1,0:T(8,128)(2,1)S(1)} %concatenate.6, s32[1024]{0:T(1024)S(1)} %fusion.21), kind=kCustom, calls=%fused_computation | custom fusion | bytes 4198400 | tf_op jit(solution)/shard_map/gather | solution.py:49
  185.7 75.9 %all-to-all-done.2 = bf16[896,3,1024]{2,1,0:T(4,128)(2,1)} async-done(((bf16[896,3,1024]{2,1,0:T(4,128)(2,1)}), bf16[896,3,1024]{2,1,0:T(4,128)(2,1)}, u32[]{:S(2)}, u32[]{:S(2)}) %all-to-all-start.2) | async-done | bytes 5505056 | tf_op jit(solution)/shard_map/all_to_all | solution.py:42
  261.6 8.7 %all-to-all-start = ((bf16[32,32,1024]{2,1,0:T(8,128)(2,1)}), bf16[32,32,1024]{2,1,0:T(8,128)(2,1)S(1)}, u32[]{:S(2)}, u32[]{:S(2)}) async-start(bf16[32,32,1024]{2,1,0:T(8,128)(2,1)} %bitcast.4), calls=%async_computation | async-start | bytes 4194304 | tf_op jit(solution)/shard_map/all_to_all | solution.py:50
  270.4 18.2 %fusion.28 = (bf16[896,1,1024]{2,1,0:T(2,128)(2,1)}, bf16[896,1,1024]{2,1,0:T(2,128)(2,1)}, bf16[896,1,1024]{2,1,0:T(2,128)(2,1)}) fusion(bf16[896,3,1024]{2,1,0:T(4,128)(2,1)} %all-to-all-done.2), kind=kLoop, calls=%fused_computation.70 | loop fusion | bytes 11010048 | tf_op jit(solution)/shard_map/slice | solution.py:57
  288.6 10.0 %all-to-all-done = bf16[32,32,1024]{2,1,0:T(8,128)(2,1)S(1)} async-done(((bf16[32,32,1024]{2,1,0:T(8,128)(2,1)}), bf16[32,32,1024]{2,1,0:T(8,128)(2,1)S(1)}, u32[]{:S(2)}, u32[]{:S(2)}) %all-to-all-start) | async-done | bytes 2097184 | tf_op jit(solution)/shard_map/all_to_all | solution.py:50
  298.6 4.6 %convert_bitcast_fusion.1 = bf16[1024,1,896]{2,0,1:T(8,128)(2,1)S(1)} fusion(bf16[1024,1024]{1,0:T(8,128)(2,1)S(1)} %bitcast.91, bf16[896,1,1024]{2,1,0:T(2,128)(2,1)} %get-tuple-element.9), kind=kOutput, calls=%fused_computation.19 | convolution fusion | flops 1879965696 | bytes 5767168 | tf_op jit(solution)/shard_map/dot_general | solution.py:24
  303.2 2.4 convert_bitcast_fusion
  305.6 2.2 pad_maximum_fusion
  307.9 44.0 %reduce-scatter.2.cloned.1.call-done = bf16[128,2,896]{2,0,1:T(8,128)(2,1)} async-done(((bf16[1024,2,896]{2,0,1:T(8,128)(2,1)}), bf16[128,2,896]{2,0,1:T(8,128)(2,1)}) %reduce-scatter.2.cloned.1.call-update) | async-done | bytes 458768 | tf_op jit(solution)/shard_map/reduce_scatter | solution.py:54
  351.9 1.1 convert_element_type.40
  353.0 0.8 fusion.13
  353.8 35.5 %all-gather.2.cloned.1.call-done = bf16[1024,896]{1,0:T(8,128)(2,1)} async-done(((bf16[128,896]{1,0:T(8,128)(2,1)}), bf16[1024,896]{1,0:T(8,128)(2,1)}) %all-gather.2.cloned.1.call-update) | async-done | bytes 1835024 | tf_op jit(solution)/shard_map/all_gather | solution.py:56
  389.3 6.3 %convolution_convert_fusion = bf16[1024,1024]{1,0:T(8,128)(2,1)} fusion(bf16[1024,896]{1,0:T(8,128)(2,1)} %all-gather.2.cloned.1.call-done, bf16[896,1,1024]{2,1,0:T(2,128)(2,1)} %get-tuple-element.7), kind=kOutput, calls=%fused_computation.9 | convolution fusion | flops 1880096768 | bytes 5767168 | tf_op jit(solution)/shard_map/dot_general | solution.py:57
  395.6 11.6 %all-to-all-start.3 = ((bf16[32,32,1024]{2,1,0:T(8,128)(2,1)}), bf16[32,32,1024]{2,1,0:T(8,128)(2,1)S(1)}, u32[]{:S(2)}, u32[]{:S(2)}) async-start(bf16[32,32,1024]{2,1,0:T(8,128)(2,1)} %bitcast.90), calls=%async_computation.4 | async-start | bytes 4194304 | tf_op jit(solution)/shard_map/all_to_all | solution.py:60
  407.2 0.1 copy.65
  407.4 0.1 reshape.119
  407.5 3.5 fusion.29
  411.1 4.5 %gather_fusion.3 = f32[512]{0:T(512)S(1)} fusion(f32[256,32]{0,1:T(8,128)S(1)} %fusion.29, s32[512]{0:T(512)S(1)} %reshape.119), kind=kCustom, calls=%fused_computation.3 | custom fusion | bytes 8192 | tf_op jit(solution)/shard_map/jit(take_along_axis)/gather | solution.py:35
  415.7 0.1 reshape.122
  415.9 0.1 copy.67
  416.1 19.6 %all-to-all-done.3 = bf16[32,32,1024]{2,1,0:T(8,128)(2,1)S(1)} async-done(((bf16[32,32,1024]{2,1,0:T(8,128)(2,1)}), bf16[32,32,1024]{2,1,0:T(8,128)(2,1)S(1)}, u32[]{:S(2)}, u32[]{:S(2)}) %all-to-all-start.3) | async-done | bytes 2097184 | tf_op jit(solution)/shard_map/all_to_all | solution.py:60
  435.7 2.8 gather_fusion.2
  438.5 2.4 reshape.94
  440.9 3.5 multiply_reduce_fusion
  (37 shorter events, 0.6 us)
Async XLA Ops:
  6.5 401.0 %copy-start = (bf16[8192,32]{0,1:T(8,128)(2,1)S(1)}, bf16[8192,32]{0,1:T(8,128)(2,1)}, u32[]{:S(2)}) copy-start(bf16[8192,32]{0,1:T(8,128)(2,1)} %param.8) | copy-start | bytes 1572868
  29.4 9.1 %copy-start.4 = (s32[448,1]{0,1:T(1,128)S(1)}, s32[448,1]{0,1:T(1,128)}, u32[]{:S(2)}) copy-start(s32[448,1]{0,1:T(1,128)} %param.12) | copy-start | bytes 5380
  29.4 74.9 %all-to-all-start.1 = ((bf16[8,2,86016]{2,1,0:T(2,128)(2,1)}), bf16[8,2,86016]{2,1,0:T(2,128)(2,1)S(1)}, u32[]{:S(2)}, u32[]{:S(2)}) async-start(bf16[8,2,86016]{2,1,0:T(2,128)(2,1)} %reshape.154), calls=%async_computation.1 | async-start | bytes 5505024 | tf_op jit(solution)/shard_map/all_to_all | solution.py:38
  166.8 7.7 %copy-start.3 = (s32[256,2]{0,1:T(2,128)S(1)}, s32[256,2]{0,1:T(2,128)}, u32[]{:S(2)}) copy-start(s32[256,2]{0,1:T(2,128)} %param.13) | copy-start | bytes 6148
  166.8 94.8 %all-to-all-start.2 = ((bf16[896,3,1024]{2,1,0:T(4,128)(2,1)}), bf16[896,3,1024]{2,1,0:T(4,128)(2,1)}, u32[]{:S(2)}, u32[]{:S(2)}) async-start(bf16[896,3,1024]{2,1,0:T(4,128)(2,1)} %gather_fusion.1), calls=%async_computation.2 | async-start | bytes 14680064 | tf_op jit(solution)/shard_map/all_to_all | solution.py:42
  261.6 37.0 %all-to-all-start = ((bf16[32,32,1024]{2,1,0:T(8,128)(2,1)}), bf16[32,32,1024]{2,1,0:T(8,128)(2,1)S(1)}, u32[]{:S(2)}, u32[]{:S(2)}) async-start(bf16[32,32,1024]{2,1,0:T(8,128)(2,1)} %bitcast.4), calls=%async_computation | async-start | bytes 4194304 | tf_op jit(solution)/shard_map/all_to_all | solution.py:50
  270.3 81.6 %reduce-scatter.2.cloned.1.call-start = ((), (), s32[]{:S(2)}) async-start(), calls=%async_computation.5 | async-start | bytes 4128768 | tf_op jit(solution)/shard_map/reduce_scatter | solution.py:54
  298.6 4.6 %copy-start.2 = (bf16[896,1,1024]{2,1,0:T(2,128)(2,1)S(1)}, bf16[896,1,1024]{2,1,0:T(2,128)(2,1)}, u32[]{:S(2)}) copy-start(bf16[896,1,1024]{2,1,0:T(2,128)(2,1)} %get-tuple-element.8) | copy-start | bytes 5505028
  307.8 81.5 %all-gather.2.cloned.1.call-start = ((), (), s32[]{:S(2)}) async-start(), calls=%async_computation.6 | async-start | bytes 2064384 | tf_op jit(solution)/shard_map/all_gather | solution.py:56
  395.6 40.1 %all-to-all-start.3 = ((bf16[32,32,1024]{2,1,0:T(8,128)(2,1)}), bf16[32,32,1024]{2,1,0:T(8,128)(2,1)S(1)}, u32[]{:S(2)}, u32[]{:S(2)}) async-start(bf16[32,32,1024]{2,1,0:T(8,128)(2,1)} %bitcast.90), calls=%async_computation.4 | async-start | bytes 4194304 | tf_op jit(solution)/shard_map/all_to_all | solution.py:60
  435.7 8.6 %copy-start.1 = (bf16[8192,32]{0,1:T(8,128)(2,1)S(1)}, bf16[8192,32]{0,1:T(8,128)(2,1)}, u32[]{:S(2)}) copy-start(bf16[8192,32]{0,1:T(8,128)(2,1)} %param.8) | copy-start | bytes 1572868
Sparse Core Ops, SparseCore 0:
  307.9 43.9 reduce-scatter.1
  353.9 35.3 all-gather.1
where the time goes:
time: 452 us; the launch traced here: 451 us
  waiting for transfers between devices  246 us (54%)
  local copies, waits for them, and re-layouts  125 us (28%)
  starting transfers between devices  37.2 us (8%)
  matrix products  16.8 us (4%)
  between operations  13.8 us (3%)
  other arithmetic  12.4 us (3%)
    all_to_all x1, waiting for transfers between devices, on_device(): own = lax.all_to_all(pick, 'dp', split_axis=0, concat_axis=0, tiled=True)  75.9 us
    all_to_all x1, waiting for transfers between devices, on_device(): lax.all_to_all(stacked, 'tensor', split_axis=2, concat_axis=0, tiled=True)  61.2 us
    reduce_scatter x1, waiting for transfers between devices, on_device(): lax.psum_scatter(both, 'tensor', scatter_dimension=0, tiled=True)  44 us
    all_gather x1, waiting for transfers between devices, on_device(): hidden = lax.all_gather(hidden_part, 'tensor', axis=0, tiled=True)  35.5 us
    gather x1, local copies, waits for them, and re-layouts, on_device(): pick = with_zero_row(rows)[unit_list]  33.1 us
    unnamed x13, local copies, waits for them, and re-layouts  25.7 us
    all_to_all x1, waiting for transfers between devices, on_device(): lax.all_to_all(expert_out, 'dp', split_axis=0, concat_axis=0, tiled=True)  19.6 us
    slice x1, local copies, waits for them, and re-layouts, on_device(): own[:, 2, :]  18.2 us
  transfers between devices with their start and end apart: 6, of which 6 were waited for; matrix products, arithmetic and copies ran while one was open for 9% of the time, Pallas kernels for 0%

commit v1 on v0

--- a/solution.py
+++ b/solution.py
@@ -35,7 +35,16 @@
     scores = jax.nn.sigmoid(jnp.take_along_axis(logits, expert_ids, axis=1))
     mixing = scores / jnp.sum(scores, axis=1, keepdims=True)
     stacked = jnp.stack([gate_weight, up_weight, down_weight], axis=1)
-    rows = lax.all_to_all(stacked, "tensor", split_axis=2, concat_axis=0, tiled=True)
+
+    def touch_view_over_axis(field_in):
+        return jnp.concatenate(
+            lax.all_to_all(
+                jnp.stack(jnp.split(field_in, lax.axis_size("tensor"), 2), 0), "tensor", 0, 0
+            ),
+            0,
+        )
+
+    rows = touch_view_over_axis(stacked)
     unit_cap = 2 * rows.shape[0] // owners
     unit_list, unit_spot = place_rows(cluster_of[:, 0], owners, unit_cap)
     pick = with_zero_row(rows)[unit_list]

time: 452 us -> 414 us (0.916)
  local copies, waits for them, and re-layouts: 125 us -> 86.7 us
    unnamed x13 -> x18, local copies, waits for them, and re-layouts: 25.7 us -> 5.52 us
    all_to_all x2 -> x1, local copies, waits for them, and re-layouts: 13 us -> 0.28 us  [touch_view_over_axis(): lax.all_to_all(jnp.stack(jnp.split(field_in, lax.axis_size('tensor'), 2),...]
    another operation x4, local copies, waits for them, and re-layouts: 8.63 us -> 0.99 us  [the longest x1 0.76 us: touch_view_over_axis(): jnp.stack(jnp.split(field_in, lax.axis_size('tensor'), 2), 0)]
    all_to_all x1, waiting for transfers between devices: 75.9 us -> 80.6 us  [on_device(): own = lax.all_to_all(pick, 'dp', split_axis=0, concat_axis=0, tiled=True)]
    all_to_all x1, waiting for transfers between devices: 61.2 us -> 56.4 us  [touch_view_over_axis(): lax.all_to_all(jnp.stack(jnp.split(field_in, lax.axis_size('tensor'), 2),...]
  transfers between devices with their start and end apart: 6 -> 6, of which waited for: 6 -> 6; matrix products, arithmetic and copies ran while one was open for 9% -> 10% of each run, Pallas kernels for 0% -> 0%
where the time goes in v1:
time: 414 us; the launch traced here: 413 us
  waiting for transfers between devices  246 us (59%)
  local copies, waits for them, and re-layouts  86.7 us (21%)
  starting transfers between devices  37.2 us (9%)
  matrix products  16.8 us (4%)
  between operations  13.7 us (3%)
  other arithmetic  12.4 us (3%)
    all_to_all x1, waiting for transfers between devices, on_device(): own = lax.all_to_all(pick, 'dp', split_axis=0, concat_axis=0, tiled=True)  80.6 us
    all_to_all x1, waiting for transfers between devices, touch_view_over_axis(): lax.all_to_all(jnp.stack(jnp.split(field_in, lax.axis_size('tensor'), 2),...  56.4 us
    reduce_scatter x1, waiting for transfers between devices, on_device(): lax.psum_scatter(both, 'tensor', scatter_dimension=0, tiled=True)  44 us
    all_gather x1, waiting for transfers between devices, on_device(): hidden = lax.all_gather(hidden_part, 'tensor', axis=0, tiled=True)  35.5 us
    gather x1, local copies, waits for them, and re-layouts, on_device(): pick = with_zero_row(rows)[unit_list]  33.1 us
    all_to_all x1, waiting for transfers between devices, on_device(): lax.all_to_all(expert_out, 'dp', split_axis=0, concat_axis=0, tiled=True)  19.6 us
    slice x1, local copies, waits for them, and re-layouts, on_device(): own[:, 2, :]  18.2 us
    all_to_all x1, starting transfers between devices, on_device(): lax.all_to_all(expert_out, 'dp', split_axis=0, concat_axis=0, tiled=True)  11.6 us
  transfers between devices with their start and end apart: 6, of which 6 were waited for; matrix products, arithmetic and copies ran while one was open for 10% of the time, Pallas kernels for 0%

profile of v1, /device:TPU:1, one launch (start us, length us, event | category | flops | bytes accessed | tf_op | source)
XLA Modules:
  0.0 413.1 jit_solution(13415604123316097258)
XLA Ops:
  6.5 2.1 pad_maximum_fusion.1
  8.6 0.7 fusion.21
  9.4 0.8 fusion.20
  10.1 0.8 fusion.19
  10.9 0.8 fusion.18
  11.7 0.8 fusion.17
  12.4 0.8 fusion.16
  13.2 0.8 fusion.15
  14.0 0.8 fusion.14
  14.8 9.1 %all-to-all-start.1 = ((bf16[8,56,3,1024]{3,1,2,0:T(8,128)(2,1)}), bf16[8,56,3,1024]{3,1,2,0:T(8,128)(2,1)S(1)}, u32[]{:S(2)}, u32[]{:S(2)}) async-start(bf16[8,56,3,1024]{3,1,2,0:T(8,128)(2,1)} %fusion.14), calls=%async_computation.1 | async-start | bytes 5505024 | tf_op jit(solution)/shard_map/all_to_all | solution.py:41
  24.0 0.1 eq.51
  24.2 0.1 eq.47
  24.3 1.2 reduce-window.14
  25.5 0.2 slice_reduce_fusion.1
  25.8 0.1 copy.62
  25.9 0.1 mul.48
  26.1 1.2 reduce-window.16
  27.3 0.2 slice_reduce_fusion
  27.7 2.4 scatter_custom_fusion
  30.3 2.9 scatter_custom_fusion.1
  33.2 56.4 %all-to-all-done.1 = bf16[8,56,3,1024]{3,1,2,0:T(8,128)(2,1)S(1)} async-done(((bf16[8,56,3,1024]{3,1,2,0:T(8,128)(2,1)}), bf16[8,56,3,1024]{3,1,2,0:T(8,128)(2,1)S(1)}, u32[]{:S(2)}, u32[]{:S(2)}) %all-to-all-start.1) | async-done | bytes 2752544 | tf_op jit(solution)/shard_map/all_to_all | solution.py:41
  89.7 0.3 copy.66
  90.0 2.4 copy.67
  92.3 3.2 concatenate.7
  95.5 33.1 %gather_fusion.1 = bf16[896,3,1024]{2,1,0:T(4,128)(2,1)} fusion(bf16[449,3,1024]{2,1,0:T(4,128)(2,1)} %concatenate.7, s32[1024]{0:T(1024)S(1)} %get-tuple-element.11), kind=kCustom, calls=%fused_computation.1 | custom fusion | bytes 11013632 | tf_op jit(solution)/shard_map/gather | solution.py:50
  128.6 7.6 %all-to-all-start.2 = ((bf16[896,3,1024]{2,1,0:T(4,128)(2,1)}), bf16[896,3,1024]{2,1,0:T(4,128)(2,1)}, u32[]{:S(2)}, u32[]{:S(2)}) async-start(bf16[896,3,1024]{2,1,0:T(4,128)(2,1)} %gather_fusion.1), calls=%async_computation.2 | async-start | bytes 14680064 | tf_op jit(solution)/shard_map/all_to_all | solution.py:51
  136.3 1.1 constant_dynamic-slice_fusion
  137.4 5.4 %gather_fusion = bf16[1024,1024]{1,0:T(8,128)(2,1)} fusion(bf16[257,1024]{1,0:T(8,128)(2,1)S(1)} %concatenate.6, s32[1024]{0:T(1024)S(1)} %get-tuple-element.10), kind=kCustom, calls=%fused_computation | custom fusion | bytes 4198400 | tf_op jit(solution)/shard_map/gather | solution.py:58
  142.8 80.6 %all-to-all-done.2 = bf16[896,3,1024]{2,1,0:T(4,128)(2,1)} async-done(((bf16[896,3,1024]{2,1,0:T(4,128)(2,1)}), bf16[896,3,1024]{2,1,0:T(4,128)(2,1)}, u32[]{:S(2)}, u32[]{:S(2)}) %all-to-all-start.2) | async-done | bytes 5505056 | tf_op jit(solution)/shard_map/all_to_all | solution.py:51
  223.4 8.7 %all-to-all-start = ((bf16[32,32,1024]{2,1,0:T(8,128)(2,1)}), bf16[32,32,1024]{2,1,0:T(8,128)(2,1)S(1)}, u32[]{:S(2)}, u32[]{:S(2)}) async-start(bf16[32,32,1024]{2,1,0:T(8,128)(2,1)} %bitcast.4), calls=%async_computation | async-start | bytes 4194304 | tf_op jit(solution)/shard_map/all_to_all | solution.py:59
  232.2 18.2 %fusion.36 = (bf16[896,1,1024]{2,1,0:T(2,128)(2,1)}, bf16[896,1,1024]{2,1,0:T(2,128)(2,1)}, bf16[896,1,1024]{2,1,0:T(2,128)(2,1)}) fusion(bf16[896,3,1024]{2,1,0:T(4,128)(2,1)} %all-to-all-done.2), kind=kLoop, calls=%fused_computation.86 | loop fusion | bytes 11010048 | tf_op jit(solution)/shard_map/slice | solution.py:66
  250.5 10.0 %all-to-all-done = bf16[32,32,1024]{2,1,0:T(8,128)(2,1)S(1)} async-done(((bf16[32,32,1024]{2,1,0:T(8,128)(2,1)}), bf16[32,32,1024]{2,1,0:T(8,128)(2,1)S(1)}, u32[]{:S(2)}, u32[]{:S(2)}) %all-to-all-start) | async-done | bytes 2097184 | tf_op jit(solution)/shard_map/all_to_all | solution.py:59
  260.5 4.6 %convert_bitcast_fusion.1 = bf16[1024,1,896]{2,0,1:T(8,128)(2,1)S(1)} fusion(bf16[1024,1024]{1,0:T(8,128)(2,1)S(1)} %bitcast.115, bf16[896,1,1024]{2,1,0:T(2,128)(2,1)} %get-tuple-element.9), kind=kOutput, calls=%fused_computation.19 | convolution fusion | flops 1879965696 | bytes 5767168 | tf_op jit(solution)/shard_map/dot_general | solution.py:24
  265.1 2.4 convert_bitcast_fusion
  267.4 2.2 pad_maximum_fusion
  269.7 44.0 %reduce-scatter.2.cloned.1.call-done = bf16[128,2,896]{2,0,1:T(8,128)(2,1)} async-done(((bf16[1024,2,896]{2,0,1:T(8,128)(2,1)}), bf16[128,2,896]{2,0,1:T(8,128)(2,1)}) %reduce-scatter.2.cloned.1.call-update) | async-done | bytes 458768 | tf_op jit(solution)/shard_map/reduce_scatter | solution.py:63
  313.7 1.1 convert_element_type.40
  314.8 0.8 fusion.13
  315.6 35.5 %all-gather.2.cloned.1.call-done = bf16[1024,896]{1,0:T(8,128)(2,1)} async-done(((bf16[128,896]{1,0:T(8,128)(2,1)}), bf16[1024,896]{1,0:T(8,128)(2,1)}) %all-gather.2.cloned.1.call-update) | async-done | bytes 1835024 | tf_op jit(solution)/shard_map/all_gather | solution.py:65
  351.1 6.3 %convolution_convert_fusion = bf16[1024,1024]{1,0:T(8,128)(2,1)} fusion(bf16[1024,896]{1,0:T(8,128)(2,1)} %all-gather.2.cloned.1.call-done, bf16[896,1,1024]{2,1,0:T(2,128)(2,1)} %get-tuple-element.7), kind=kOutput, calls=%fused_computation.9 | convolution fusion | flops 1880096768 | bytes 5767168 | tf_op jit(solution)/shard_map/dot_general | solution.py:66
  357.4 11.6 %all-to-all-start.3 = ((bf16[32,32,1024]{2,1,0:T(8,128)(2,1)}), bf16[32,32,1024]{2,1,0:T(8,128)(2,1)S(1)}, u32[]{:S(2)}, u32[]{:S(2)}) async-start(bf16[32,32,1024]{2,1,0:T(8,128)(2,1)} %bitcast.114), calls=%async_computation.4 | async-start | bytes 4194304 | tf_op jit(solution)/shard_map/all_to_all | solution.py:69
  369.2 0.1 reshape.123
  369.4 3.5 fusion.37
  372.9 4.5 %gather_fusion.3 = f32[512]{0:T(512)S(1)} fusion(f32[256,32]{0,1:T(8,128)S(1)} %fusion.37, s32[512]{0:T(512)S(1)} %reshape.123), kind=kCustom, calls=%fused_computation.3 | custom fusion | bytes 8192 | tf_op jit(solution)/shard_map/jit(take_along_axis)/gather | solution.py:35
  377.9 19.6 %all-to-all-done.3 = bf16[32,32,1024]{2,1,0:T(8,128)(2,1)S(1)} async-done(((bf16[32,32,1024]{2,1,0:T(8,128)(2,1)}), bf16[32,32,1024]{2,1,0:T(8,128)(2,1)S(1)}, u32[]{:S(2)}, u32[]{:S(2)}) %all-to-all-start.3) | async-done | bytes 2097184 | tf_op jit(solution)/shard_map/all_to_all | solution.py:69
  397.6 2.8 gather_fusion.2
  400.4 2.4 reshape.98
  402.7 3.5 multiply_reduce_fusion
  (41 shorter events, 1.2 us)
Async XLA Ops:
  6.5 362.8 %copy-start = (bf16[8192,32]{0,1:T(8,128)(2,1)S(1)}, bf16[8192,32]{0,1:T(8,128)(2,1)}, u32[]{:S(2)}) copy-start(bf16[8192,32]{0,1:T(8,128)(2,1)} %param.8) | copy-start | bytes 1572868
  14.8 9.1 %copy-start.3 = (s32[256,2]{0,1:T(2,128)S(1)}, s32[256,2]{0,1:T(2,128)}, u32[]{:S(2)}) copy-start(s32[256,2]{0,1:T(2,128)} %param.13) | copy-start | bytes 6148
  14.8 11.3 %copy-start.4 = (s32[448,1]{0,1:T(1,128)S(1)}, s32[448,1]{0,1:T(1,128)}, u32[]{:S(2)}) copy-start(s32[448,1]{0,1:T(1,128)} %param.12) | copy-start | bytes 5380
  14.8 74.9 %all-to-all-start.1 = ((bf16[8,56,3,1024]{3,1,2,0:T(8,128)(2,1)}), bf16[8,56,3,1024]{3,1,2,0:T(8,128)(2,1)S(1)}, u32[]{:S(2)}, u32[]{:S(2)}) async-start(bf16[8,56,3,1024]{3,1,2,0:T(8,128)(2,1)} %fusion.14), calls=%async_computation.1 | async-start | bytes 5505024 | tf_op jit(solution)/shard_map/all_to_all | solution.py:41
  128.6 94.8 %all-to-all-start.2 = ((bf16[896,3,1024]{2,1,0:T(4,128)(2,1)}), bf16[896,3,1024]{2,1,0:T(4,128)(2,1)}, u32[]{:S(2)}, u32[]{:S(2)}) async-start(bf16[896,3,1024]{2,1,0:T(4,128)(2,1)} %gather_fusion.1), calls=%async_computation.2 | async-start | bytes 14680064 | tf_op jit(solution)/shard_map/all_to_all | solution.py:51
  223.4 37.0 %all-to-all-start = ((bf16[32,32,1024]{2,1,0:T(8,128)(2,1)}), bf16[32,32,1024]{2,1,0:T(8,128)(2,1)S(1)}, u32[]{:S(2)}, u32[]{:S(2)}) async-start(bf16[32,32,1024]{2,1,0:T(8,128)(2,1)} %bitcast.4), calls=%async_computation | async-start | bytes 4194304 | tf_op jit(solution)/shard_map/all_to_all | solution.py:59
  232.2 81.6 %reduce-scatter.2.cloned.1.call-start = ((), (), s32[]{:S(2)}) async-start(), calls=%async_computation.5 | async-start | bytes 4128768 | tf_op jit(solution)/shard_map/reduce_scatter | solution.py:63
  260.5 4.6 %copy-start.2 = (bf16[896,1,1024]{2,1,0:T(2,128)(2,1)S(1)}, bf16[896,1,1024]{2,1,0:T(2,128)(2,1)}, u32[]{:S(2)}) copy-start(bf16[896,1,1024]{2,1,0:T(2,128)(2,1)} %get-tuple-element.8) | copy-start | bytes 5505028
  269.6 81.5 %all-gather.2.cloned.1.call-start = ((), (), s32[]{:S(2)}) async-start(), calls=%async_computation.6 | async-start | bytes 2064384 | tf_op jit(solution)/shard_map/all_gather | solution.py:65
  357.4 40.1 %all-to-all-start.3 = ((bf16[32,32,1024]{2,1,0:T(8,128)(2,1)}), bf16[32,32,1024]{2,1,0:T(8,128)(2,1)S(1)}, u32[]{:S(2)}, u32[]{:S(2)}) async-start(bf16[32,32,1024]{2,1,0:T(8,128)(2,1)} %bitcast.114), calls=%async_computation.4 | async-start | bytes 4194304 | tf_op jit(solution)/shard_map/all_to_all | solution.py:69
  397.6 8.6 %copy-start.1 = (bf16[8192,32]{0,1:T(8,128)(2,1)S(1)}, bf16[8192,32]{0,1:T(8,128)(2,1)}, u32[]{:S(2)}) copy-start(bf16[8192,32]{0,1:T(8,128)(2,1)} %param.8) | copy-start | bytes 1572868
Sparse Core Ops, SparseCore 0:
  269.8 43.9 reduce-scatter.1
  315.8 35.3 all-gather.1
